TPU v7x, 32 devices: a whole 2x2x4 slice. The times are simulated.
32 devices in a mesh: ctx: 8 (over y, x, core), head: 4 (over z).
Axes of the slice: x: 2, y: 2, z: 4, core: 2. Of those that a mesh axis runs over, the one named last changes fastest.
Arguments:
- queries: bfloat16 [4096, 4096], P(('ctx', 'head')), may hold values from -42 to 42
- keys: bfloat16 [4096, 1024], P(('ctx', 'head')), may hold values from -4 to 4
- values: bfloat16 [4096, 1024], P(('ctx', 'head')), may hold values from -6 to 6
- out_grad: bfloat16 [4096, 4096], P(('ctx', 'head')), may hold values from -6 to 6
- beacon_pos: int32 [8, 64], P('ctx'), may hold values from 0 to 511, as said below
Outputs:
- attended: bfloat16 [4096, 4096], P(('ctx', 'head'))
- query_grad: bfloat16 [4096, 4096], P(('ctx', 'head'))
- key_grad: bfloat16 [4096, 1024], P(('ctx', 'head'))
- value_grad: bfloat16 [4096, 1024], P(('ctx', 'head'))
Inputs may be any that keep to these rules, and one draw needn't show every extreme that they name: `beacon_pos`: row c holds 64 distinct positions in increasing order, the first equal to 0 and the last equal to 511.
All inputs are finite; a program needn't handle non-finite values.
Results may differ from a plain program's by a relative error of at most 0.029.
Values may be sent and summed in bfloat16 or wider, within the bound.
No kernel may reach another device: no remote copies, remote signals or barrier semaphores. Data moves between devices by JAX's collectives and lax.ppermute only.
A program may use at most 128 MiB of HBM per device.

v0:
```python
import jax
import jax.numpy as jnp
from jax import lax
from jax.sharding import PartitionSpec as P

HD = 128
NEG_FILL = -1e30


def local(queries, keys, values, out_grad, beacon_pos):
    query_rows, key_rows, value_rows, grad_rows = (
        lax.all_to_all(queries, "head", split_axis=1, concat_axis=0, tiled=True),
        lax.all_to_all(keys, "head", split_axis=1, concat_axis=0, tiled=True),
        lax.all_to_all(values, "head", split_axis=1, concat_axis=0, tiled=True),
        lax.all_to_all(out_grad, "head", split_axis=1, concat_axis=0, tiled=True),
    )
    window = query_rows.shape[0]
    kv_local = key_rows.shape[1] // HD
    group_size = query_rows.shape[1] // HD // kv_local
    scaling = HD ** (-0.5)
    query_head_rows = query_rows.reshape(window, kv_local, group_size, HD)
    head_gradients = grad_rows.reshape(window, kv_local, group_size, HD)
    key_heads = key_rows.reshape(window, kv_local, HD)
    value_heads = value_rows.reshape(window, kv_local, HD)
    positions = beacon_pos[0]
    beacon_keys, beacon_values = (
        lax.all_gather(key_rows[positions], "ctx", axis=0, tiled=True),
        lax.all_gather(value_rows[positions], "ctx", axis=0, tiled=True),
    )
    beacon_total = beacon_keys.shape[0]
    per_shard = positions.shape[0]
    beacon_key_heads = beacon_keys.reshape(beacon_total, kv_local, HD)
    beacon_value_heads = beacon_values.reshape(beacon_total, kv_local, HD)
    owners = jnp.arange(beacon_total, dtype=jnp.int32) // per_shard
    shard_id = lax.axis_index("ctx")
    block_rows = min(beacon_total, 512)
    block_count = beacon_total // block_rows
    causal = jnp.arange(window)[:, None] >= jnp.arange(window)[None, :]
    local_scores = (
        jnp.einsum("wkgd,vkd->kgwv", query_head_rows, key_heads, preferred_element_type=jnp.float32)
        * scaling
    )
    local_scores = jnp.where(causal, local_scores, NEG_FILL)

    def beacon_scores(block_index):
        start = block_index * block_rows
        key_tile_block = lax.dynamic_slice_in_dim(beacon_key_heads, start, block_rows, 0)
        value_tile_block = lax.dynamic_slice_in_dim(beacon_value_heads, start, block_rows, 0)
        seen = lax.dynamic_slice_in_dim(owners, start, block_rows, 0) < shard_id
        scores = (
            jnp.einsum(
                "jahm,pam->ahjp",
                query_head_rows,
                key_tile_block,
                preferred_element_type=jnp.float32,
            )
            * scaling
        )
        return (jnp.where(seen, scores, NEG_FILL), key_tile_block, value_tile_block, start)

    row_max = jnp.max(local_scores, axis=-1)
    row_sum = jnp.sum(jnp.exp(local_scores - row_max[..., None]), axis=-1)

    def gather_stats(block_index, stats):
        old_max, old_sum = stats
        scores = beacon_scores(block_index)[0]
        new_max = jnp.maximum(old_max, jnp.max(scores, axis=-1))
        updated_sum = old_sum * jnp.exp(old_max - new_max) + jnp.sum(
            jnp.exp(scores - new_max[..., None]), axis=-1
        )
        return (new_max, updated_sum)

    row_max, row_sum = lax.fori_loop(0, block_count, gather_stats, (row_max, row_sum))

    def normalize(scores):
        return jnp.exp(scores - row_max[..., None]) / row_sum[..., None]

    local_probs = normalize(local_scores)
    local_probs_low = local_probs.astype(jnp.bfloat16)
    attended = jnp.einsum(
        "kgwv,vkd->wkgd", local_probs_low, value_heads, preferred_element_type=jnp.float32
    )

    def add_values(block_index, running):
        scores, key_tile_block, value_tile_block, start = beacon_scores(block_index)
        reduced_probability = normalize(scores).astype(jnp.bfloat16)
        return running + jnp.einsum(
            "lupa,alx->plux",
            reduced_probability,
            value_tile_block,
            preferred_element_type=jnp.float32,
        )

    attended = lax.fori_loop(0, block_count, add_values, attended).astype(jnp.bfloat16)
    row_dot = jnp.einsum(
        "wkgd,wkgd->kgw", head_gradients, attended, preferred_element_type=jnp.float32
    )[..., None]
    local_dprob = jnp.einsum(
        "wkgd,vkd->kgwv", head_gradients, value_heads, preferred_element_type=jnp.float32
    )
    local_grad_scores = (local_probs * (local_dprob - row_dot)).astype(jnp.bfloat16)
    query_grad = jnp.einsum(
        "kgwv,vkd->wkgd", local_grad_scores, key_heads, preferred_element_type=jnp.float32
    )
    key_grad = (
        jnp.einsum(
            "kgwv,wkgd->vkd", local_grad_scores, query_head_rows, preferred_element_type=jnp.float32
        )
        * scaling
    )
    value_grad = jnp.einsum(
        "kgwv,wkgd->vkd", local_probs_low, head_gradients, preferred_element_type=jnp.float32
    )

    def add_grads(block_index, carried):
        query_count_total, key_buffer, value_buffer = carried
        scores, key_tile_block, value_tile_block, start = beacon_scores(block_index)
        probabilities = normalize(scores)
        reduced_probability = probabilities.astype(jnp.bfloat16)
        dprob = jnp.einsum(
            "jahm,pam->ahjp", head_gradients, value_tile_block, preferred_element_type=jnp.float32
        )
        score_gradient = (probabilities * (dprob - row_dot)).astype(jnp.bfloat16)
        query_count_total = query_count_total + jnp.einsum(
            "lupa,alx->plux", score_gradient, key_tile_block, preferred_element_type=jnp.float32
        )
        key_part = (
            jnp.einsum(
                "ecxr,xecz->rez",
                score_gradient,
                query_head_rows,
                preferred_element_type=jnp.float32,
            )
            * scaling
        )
        value_part = jnp.einsum(
            "ecxr,xecz->rez",
            reduced_probability,
            head_gradients,
            preferred_element_type=jnp.float32,
        )
        key_buffer = lax.dynamic_update_slice_in_dim(key_buffer, key_part, start, 0)
        value_buffer = lax.dynamic_update_slice_in_dim(value_buffer, value_part, start, 0)
        return (query_count_total, key_buffer, value_buffer)

    empty_buffer = jnp.zeros((beacon_total, kv_local, HD), jnp.float32)
    query_grad, key_buffer, value_buffer = lax.fori_loop(
        0, block_count, add_grads, (query_grad, empty_buffer, empty_buffer)
    )
    query_grad = (query_grad * scaling).astype(jnp.bfloat16)
    own_keys, own_values = (
        lax.psum_scatter(
            key_buffer.astype(jnp.bfloat16), "ctx", scatter_dimension=0, tiled=True
        ).astype(jnp.float32),
        lax.psum_scatter(
            value_buffer.astype(jnp.bfloat16), "ctx", scatter_dimension=0, tiled=True
        ).astype(jnp.float32),
    )
    key_grad = key_grad.at[positions].add(own_keys)
    value_grad = value_grad.at[positions].add(own_values)
    attended_out = attended.reshape(window, group_size * kv_local * HD)
    query_out = query_grad.reshape(window, group_size * kv_local * HD)
    key_out = key_grad.astype(jnp.bfloat16).reshape(window, kv_local * HD)
    value_out = value_grad.astype(jnp.bfloat16).reshape(window, kv_local * HD)
    return (
        lax.all_to_all(attended_out, "head", split_axis=0, concat_axis=1, tiled=True),
        lax.all_to_all(query_out, "head", split_axis=0, concat_axis=1, tiled=True),
        lax.all_to_all(key_out, "head", split_axis=0, concat_axis=1, tiled=True),
        lax.all_to_all(value_out, "head", split_axis=0, concat_axis=1, tiled=True),
    )


def solution(mesh):
    in_specs = (
        P(("ctx", "head"), None),
        P(("ctx", "head"), None),
        P(("ctx", "head"), None),
        P(("ctx", "head"), None),
        P("ctx", None),
    )
    out_specs = (
        P(("ctx", "head"), None),
        P(("ctx", "head"), None),
        P(("ctx", "head"), None),
        P(("ctx", "head"), None),
    )
    return jax.shard_map(local, mesh=mesh, in_specs=in_specs, out_specs=out_specs, check_vma=False)
```

profile of v0, /device:TPU:0, one launch (start us, length us, event | category | flops | bytes accessed | tf_op | source)
XLA Modules:
  0.0 285.3 jit_solution(10834364162672158835)
XLA Ops:
  8.8 6.3 %all-to-all-start = ((bf16[128,4,256]{2,0,1:T(8,128)(2,1)}), bf16[128,4,256]{2,0,1:T(8,128)(2,1)S(1)}, u32[]{:S(2)}, u32[]{:S(2)}) async-start(bf16[128,4,256]{2,0,1:T(8,128)(2,1)} %bitcast.156), calls=%async_computation | async-start | bytes 524288 | tf_op jit(solution)/shard_map/all_to_all | solution.py:13
  16.8 7.2 %all-to-all-done = bf16[128,4,256]{2,0,1:T(8,128)(2,1)S(1)} async-done(((bf16[128,4,256]{2,0,1:T(8,128)(2,1)}), bf16[128,4,256]{2,0,1:T(8,128)(2,1)S(1)}, u32[]{:S(2)}, u32[]{:S(2)}) %all-to-all-start) | async-done | bytes 262176 | tf_op jit(solution)/shard_map/all_to_all | solution.py:13
  29.8 4.7 %all-to-all-done.2 = bf16[128,4,256]{2,0,1:T(8,128)(2,1)S(1)} async-done(((bf16[128,4,256]{2,0,1:T(8,128)(2,1)}), bf16[128,4,256]{2,0,1:T(8,128)(2,1)S(1)}, u32[]{:S(2)}, u32[]{:S(2)}) %all-to-all-start.2) | async-done | bytes 262176 | tf_op jit(solution)/shard_map/all_to_all | solution.py:14
  34.5 3.5 %all-to-all-start.1 = ((bf16[128,4,1024]{2,0,1:T(8,128)(2,1)}), bf16[128,4,1024]{2,0,1:T(8,128)(2,1)S(1)}, u32[]{:S(2)}, u32[]{:S(2)}) async-start(bf16[128,4,1024]{2,0,1:T(8,128)(2,1)} %bitcast.154), calls=%async_computation.1 | async-start | bytes 2097152 | tf_op jit(solution)/shard_map/all_to_all | solution.py:12
  40.3 20.7 %all-to-all-done.1 = bf16[128,4,1024]{2,0,1:T(8,128)(2,1)S(1)} async-done(((bf16[128,4,1024]{2,0,1:T(8,128)(2,1)}), bf16[128,4,1024]{2,0,1:T(8,128)(2,1)S(1)}, u32[]{:S(2)}, u32[]{:S(2)}) %all-to-all-start.1) | async-done | bytes 1048608 | tf_op jit(solution)/shard_map/all_to_all | solution.py:12
  61.0 3.5 %all-to-all-start.4 = ((bf16[128,4,1024]{2,0,1:T(8,128)(2,1)}), bf16[128,4,1024]{2,0,1:T(8,128)(2,1)S(1)}, u32[]{:S(2)}, u32[]{:S(2)}) async-start(bf16[128,4,1024]{2,0,1:T(8,128)(2,1)} %bitcast.153), calls=%async_computation.4 | async-start | bytes 2097152 | tf_op jit(solution)/shard_map/all_to_all | solution.py:15
  66.1 9.3 %all-gather = bf16[512,256]{1,0:T(8,128)(2,1)S(1)} all-gather(bf16[64,256]{1,0:T(8,128)(2,1)S(1)} %gather_fusion), channel_id=2, replica_groups=mesh['ctx'=8,'head'=4] {'ctx'}, dimensions={0}, use_global_device_ids=true | all-gather | bytes 294912 | tf_op jit(solution)/shard_map/all_gather | solution.py:27
  77.0 9.3 %all-gather.1 = bf16[512,256]{1,0:T(8,128)(2,1)S(1)} all-gather(bf16[64,256]{1,0:T(8,128)(2,1)S(1)} %gather_fusion.1), channel_id=3, replica_groups=mesh['ctx'=8,'head'=4] {'ctx'}, dimensions={0}, use_global_device_ids=true | all-gather | bytes 294912 | tf_op jit(solution)/shard_map/all_gather | solution.py:28
  100.2 3.5 %fusion.21 = f32[512,2,128]{2,0,1:T(8,128)} fusion(bf16[512,2,4,128]{3,2,1,0:T(4,128)(2,1)S(1)} %reshape.114, f32[2,512,512,4]{2,1,3,0:T(8,128)S(1)} %get-tuple-element.77, f32[2,4,512]{2,1,0:T(4,128)S(1)} %bitcast.189, f32[2,4,512]{2,1,0:T(4,128)S(1)} %max.11, pred[512,512]{0,1:T(8,128)(4,1)S(1)} %copy-done.6), kind=kOutput, calls=%fused_computation.34 | convolution fusion | flops 547356672 | bytes 10256384 | tf_op jit(solution)/shard_map/kgwv,wkgd->vkd/dot_general | solution.py:111
  105.7 5.3 %fusion.13 = f32[2,128,4,512]{1,3,2,0:T(8,128)S(1)} fusion(bf16[512,2,128,1]{0,2,3,1:T(8,128)(2,1)S(1)} %bitcast.174, f32[2,4,512,512]{2,3,1,0:T(8,128)} %copy-done), kind=kOutput, calls=%fused_computation.28 | convolution fusion | flops 538968064 | bytes 10747904 | tf_op jit(solution)/shard_map/while/body/eval_jaxpr/lupa,alx->plux/dot_general | solution.py:87
  111.4 4.0 %bitcast_convert_fusion = (f32[2,4,512,128]{3,2,1,0:T(8,128)S(1)}, bf16[512,2,4,128]{3,0,2,1:T(8,128)(2,1)}) fusion(f32[2,128,4,512]{1,3,2,0:T(8,128)S(1)} %fusion.13, bf16[512,2,128,1]{2,1,0,3:T(2,128)(2,1)S(1)} %bitcast.184, f32[2,4,512]{2,1,0:T(4,128)S(1)} %bitcast.190, f32[2,4,512]{2,1,0:T(4,128)S(1)} %max.11, f32[2,512,512,4]{2,1,3,0:T(8,128)S(1)} %copy-done.2, ...), kind=kOutput, calls=%fused_computation.47 | convolution fusion | flops 548929536 | bytes 14188544 | tf_op jit(solution)/shard_map/kgwv,vkd->wkgd/dot_general | solution.py:80
  117.7 6.8 %fusion.3 = bf16[2,4,512,512]{2,3,1,0:T(8,128)(2,1)} fusion(f32[2,4,512]{2,1,0:T(4,128)S(1)} %copy.112, bf16[512,2,4,128]{3,2,1,0:T(4,128)(2,1)S(1)} %reshape.114, bf16[512,2,128,1]{2,1,0,3:T(2,128)(2,1)} %bitcast.183, f32[2,4,512]{2,1,0:T(4,128)S(1)} %bitcast.191, f32[2,4,512]{2,1,0:T(4,128)S(1)} %max.11, f32[2,512,512,4]{2,1,3,0:T(8,128)} %copy-done.1, ...), kind=kOutput, calls=%fused_computation.9 | convolution fusion | flops 551550976 | bytes 14204928 | tf_op jit(solution)/shard_map/wkgd,vkd->kgwv/dot_general | solution.py:98
  124.5 6.7 %fusion.1 = bf16[2,4,512,512]{2,3,1,0:T(8,128)(2,1)} fusion(f32[2,4,512,512]{2,3,1,0:T(8,128)} %copy-done, f32[2,4,512]{2,1,0:T(4,128)S(1)} %copy.112, bf16[512,2,128,1]{0,2,3,1:T(8,128)(2,1)S(1)} %bitcast.175, bf16[512,2,4,128]{3,2,1,0:T(4,128)(2,1)S(1)} %reshape.114), kind=kOutput, calls=%fused_computation.6 | convolution fusion | flops 543162368 | bytes 13910016 | tf_op jit(solution)/shard_map/while/body/eval_jaxpr/jahm,pam->ahjp/dot_general | solution.py:120
  131.7 4.1 %fusion.37 = bf16[512,2,128]{2,0,1:T(8,128)(2,1)} fusion(bf16[2,4,512,512]{2,3,1,0:T(8,128)(2,1)} %fusion.1, bf16[512,2,4,128]{3,2,1,0:T(4,128)(2,1)S(1)} %reshape.110), kind=kOutput, calls=%fused_computation.44 | convolution fusion | flops 537133056 | bytes 5505024 | tf_op jit(solution)/shard_map/while/body/eval_jaxpr/ecxr,xecz->rez/dot_general | solution.py:128
  135.9 28.9 %reduce-scatter.5.cloned.1.call-done = bf16[64,2,128]{2,0,1:T(8,128)(2,1)} async-done(((bf16[512,2,128]{2,0,1:T(8,128)(2,1)}), bf16[64,2,128]{2,0,1:T(8,128)(2,1)}) %reduce-scatter.5.cloned.1.call-update) | async-done | bytes 32784 | tf_op jit(solution)/shard_map/reduce_scatter | solution.py:155
  169.4 4.6 %all-to-all-start.7 = ((bf16[4,128,256]{2,1,0:T(8,128)(2,1)}), bf16[4,128,256]{2,1,0:T(8,128)(2,1)}, u32[]{:S(2)}, u32[]{:S(2)}) async-start(bf16[4,128,256]{2,1,0:T(8,128)(2,1)} %all_to_all.134), calls=%async_computation.9 | async-start | bytes 524288 | tf_op jit(solution)/shard_map/all_to_all | solution.py:169
  174.0 3.6 %fusion.28 = f32[512,2,128]{2,0,1:T(8,128)S(1)} fusion(bf16[2,4,512,512]{2,3,1,0:T(8,128)(2,1)} %fusion.3, bf16[512,2,4,128]{3,2,1,0:T(4,128)(2,1)S(1)} %reshape.110), kind=kOutput, calls=%fused_computation.39 | convolution fusion | flops 537001984 | bytes 5767168 | tf_op jit(solution)/shard_map/kgwv,wkgd->vkd/dot_general | solution.py:106
  179.8 22.4 %reduce-scatter.3.cloned.1.call-done = bf16[64,2,128]{2,0,1:T(8,128)(2,1)} async-done(((bf16[512,2,128]{2,0,1:T(8,128)(2,1)}), bf16[64,2,128]{2,0,1:T(8,128)(2,1)}) %reduce-scatter.3.cloned.1.call-update) | async-done | bytes 32784 | tf_op jit(solution)/shard_map/reduce_scatter | solution.py:152
  206.9 4.8 %all-to-all-start.6 = ((bf16[4,128,256]{2,1,0:T(8,128)(2,1)}), bf16[4,128,256]{2,1,0:T(8,128)(2,1)}, u32[]{:S(2)}, u32[]{:S(2)}) async-start(bf16[4,128,256]{2,1,0:T(8,128)(2,1)} %all_to_all.130), calls=%async_computation.7 | async-start | bytes 524288 | tf_op jit(solution)/shard_map/all_to_all | solution.py:168
  211.6 3.9 %fusion.9 = bf16[512,2,4,128]{3,0,2,1:T(8,128)(2,1)S(1)} fusion(f32[2,4,512,128]{3,2,1,0:T(8,128)S(1)} %fusion.50, bf16[512,2,128,1]{0,2,3,1:T(8,128)(2,1)S(1)} %bitcast.173, bf16[2,4,512,512]{2,3,1,0:T(8,128)(2,1)} %fusion.1), kind=kOutput, calls=%fused_computation.22 | convolution fusion | flops 538443776 | bytes 7602176 | tf_op jit(solution)/shard_map/while/body/eval_jaxpr/lupa,alx->plux/dot_general | solution.py:124
  220.1 3.8 %all-to-all-start.5 = ((bf16[4,128,1024]{2,1,0:T(8,128)(2,1)}), bf16[4,128,1024]{2,1,0:T(8,128)(2,1)S(1)}, u32[]{:S(2)}, u32[]{:S(2)}) async-start(bf16[4,128,1024]{2,1,0:T(8,128)(2,1)} %all_to_all.126), calls=%async_computation.5 | async-start | bytes 2097152 | tf_op jit(solution)/shard_map/all_to_all | solution.py:167
  226.3 21.5 %all-to-all-done.5 = bf16[4,128,1024]{2,1,0:T(8,128)(2,1)S(1)} async-done(((bf16[4,128,1024]{2,1,0:T(8,128)(2,1)}), bf16[4,128,1024]{2,1,0:T(8,128)(2,1)S(1)}, u32[]{:S(2)}, u32[]{:S(2)}) %all-to-all-start.5) | async-done | bytes 1048608 | tf_op jit(solution)/shard_map/all_to_all | solution.py:167
  247.8 3.5 %all-to-all-start.3 = ((bf16[4,128,1024]{2,1,0:T(8,128)(2,1)}), bf16[4,128,1024]{2,1,0:T(8,128)(2,1)S(1)}, u32[]{:S(2)}, u32[]{:S(2)}) async-start(bf16[4,128,1024]{2,1,0:T(8,128)(2,1)} %all_to_all.119), calls=%async_computation.3 | async-start | bytes 2097152 | tf_op jit(solution)/shard_map/all_to_all | solution.py:166
  256.7 19.9 %all-to-all-done.3 = bf16[4,128,1024]{2,1,0:T(8,128)(2,1)S(1)} async-done(((bf16[4,128,1024]{2,1,0:T(8,128)(2,1)}), bf16[4,128,1024]{2,1,0:T(8,128)(2,1)S(1)}, u32[]{:S(2)}, u32[]{:S(2)}) %all-to-all-start.3) | async-done | bytes 1048608 | tf_op jit(solution)/shard_map/all_to_all | solution.py:166
  (77 shorter events, 59.0 us)
Async XLA Ops:
  7.2 57.4 %copy-start.10 = (s32[1,64]{1,0:T(1,128)S(1)}, s32[1,64]{1,0:T(1,128)}, u32[]{:S(2)}) copy-start(s32[1,64]{1,0:T(1,128)} %param.9) | copy-start | bytes 772
  8.8 15.2 %all-to-all-start = ((bf16[128,4,256]{2,0,1:T(8,128)(2,1)}), bf16[128,4,256]{2,0,1:T(8,128)(2,1)S(1)}, u32[]{:S(2)}, u32[]{:S(2)}) async-start(bf16[128,4,256]{2,0,1:T(8,128)(2,1)} %bitcast.156), calls=%async_computation | async-start | bytes 524288 | tf_op jit(solution)/shard_map/all_to_all | solution.py:13
  24.1 10.4 %all-to-all-start.2 = ((bf16[128,4,256]{2,0,1:T(8,128)(2,1)}), bf16[128,4,256]{2,0,1:T(8,128)(2,1)S(1)}, u32[]{:S(2)}, u32[]{:S(2)}) async-start(bf16[128,4,256]{2,0,1:T(8,128)(2,1)} %bitcast.155), calls=%async_computation.2 | async-start | bytes 524288 | tf_op jit(solution)/shard_map/all_to_all | solution.py:14
  34.5 26.5 %all-to-all-start.1 = ((bf16[128,4,1024]{2,0,1:T(8,128)(2,1)}), bf16[128,4,1024]{2,0,1:T(8,128)(2,1)S(1)}, u32[]{:S(2)}, u32[]{:S(2)}) async-start(bf16[128,4,1024]{2,0,1:T(8,128)(2,1)} %bitcast.154), calls=%async_computation.1 | async-start | bytes 2097152 | tf_op jit(solution)/shard_map/all_to_all | solution.py:12
  61.0 28.4 %all-to-all-start.4 = ((bf16[128,4,1024]{2,0,1:T(8,128)(2,1)}), bf16[128,4,1024]{2,0,1:T(8,128)(2,1)S(1)}, u32[]{:S(2)}, u32[]{:S(2)}) async-start(bf16[128,4,1024]{2,0,1:T(8,128)(2,1)} %bitcast.153), calls=%async_computation.4 | async-start | bytes 2097152 | tf_op jit(solution)/shard_map/all_to_all | solution.py:15
  64.5 100.3 %reduce-scatter.5.cloned.1.call-start = ((), (), s32[]{:S(2)}) async-start(), calls=%async_computation.11 | async-start | bytes 294912 | tf_op jit(solution)/shard_map/reduce_scatter | solution.py:155
  90.1 2.2 copy-start.5
  90.1 2.2 copy-start.6
  94.0 6.1 %copy-start.1 = (f32[2,512,512,4]{2,1,3,0:T(8,128)}, f32[2,512,512,4]{2,1,3,0:T(8,128)S(1)}, u32[]{:S(2)}) copy-start(f32[2,512,512,4]{2,1,3,0:T(8,128)S(1)} %get-tuple-element.77) | copy-start | bytes 25165828
  100.1 3.6 %copy-start = (f32[2,4,512,512]{2,3,1,0:T(8,128)}, f32[2,4,512,512]{2,3,1,0:T(8,128)S(1)}, u32[]{:S(2)}) copy-start(f32[2,4,512,512]{2,3,1,0:T(8,128)S(1)} %fusion.6) | copy-start | bytes 25165828
  103.7 2.0 copy-start.4
  103.7 7.3 %copy-start.9 = (bf16[512,2,128]{2,1,0:T(2,128)(2,1)S(1)}, bf16[512,2,128]{2,1,0:T(2,128)(2,1)}, u32[]{:S(2)}) copy-start(bf16[512,2,128]{2,1,0:T(2,128)(2,1)} %reshape.112) | copy-start | bytes 786436
  105.7 5.8 %copy-start.2 = (f32[2,512,512,4]{2,1,3,0:T(8,128)S(1)}, f32[2,512,512,4]{2,1,3,0:T(8,128)}, u32[]{:S(2)}) copy-start(f32[2,512,512,4]{2,1,3,0:T(8,128)} %copy-done.1) | copy-start | bytes 25165828
  124.5 6.8 %copy-start.8 = (f32[512,2,128]{2,0,1:T(8,128)S(1)}, f32[512,2,128]{2,0,1:T(8,128)}, u32[]{:S(2)}) copy-start(f32[512,2,128]{2,0,1:T(8,128)} %fusion.21) | copy-start | bytes 1572868
  131.2 71.0 %reduce-scatter.3.cloned.1.call-start = ((), (), s32[]{:S(2)}) async-start(), calls=%async_computation.10 | async-start | bytes 294912 | tf_op jit(solution)/shard_map/reduce_scatter | solution.py:152
  169.4 37.5 %all-to-all-start.7 = ((bf16[4,128,256]{2,1,0:T(8,128)(2,1)}), bf16[4,128,256]{2,1,0:T(8,128)(2,1)}, u32[]{:S(2)}, u32[]{:S(2)}) async-start(bf16[4,128,256]{2,1,0:T(8,128)(2,1)} %all_to_all.134), calls=%async_computation.9 | async-start | bytes 524288 | tf_op jit(solution)/shard_map/all_to_all | solution.py:169
  174.0 4.0 %copy-start.3 = (bf16[2,4,512,512]{2,3,1,0:T(8,128)(2,1)S(1)}, bf16[2,4,512,512]{2,3,1,0:T(8,128)(2,1)}, u32[]{:S(2)}) copy-start(bf16[2,4,512,512]{2,3,1,0:T(8,128)(2,1)} %fusion.3) | copy-start | bytes 12582916
  206.9 17.0 %copy-start.7 = (bf16[512,2,4,128]{3,0,2,1:T(8,128)(2,1)S(1)}, bf16[512,2,4,128]{3,0,2,1:T(8,128)(2,1)}, u32[]{:S(2)}) copy-start(bf16[512,2,4,128]{3,0,2,1:T(8,128)(2,1)} %get-tuple-element.81) | copy-start | bytes 3145732
  206.9 13.2 %all-to-all-start.6 = ((bf16[4,128,256]{2,1,0:T(8,128)(2,1)}), bf16[4,128,256]{2,1,0:T(8,128)(2,1)}, u32[]{:S(2)}, u32[]{:S(2)}) async-start(bf16[4,128,256]{2,1,0:T(8,128)(2,1)} %all_to_all.130), calls=%async_computation.7 | async-start | bytes 524288 | tf_op jit(solution)/shard_map/all_to_all | solution.py:168
  220.1 27.7 %all-to-all-start.5 = ((bf16[4,128,1024]{2,1,0:T(8,128)(2,1)}), bf16[4,128,1024]{2,1,0:T(8,128)(2,1)S(1)}, u32[]{:S(2)}, u32[]{:S(2)}) async-start(bf16[4,128,1024]{2,1,0:T(8,128)(2,1)} %all_to_all.126), calls=%async_computation.5 | async-start | bytes 2097152 | tf_op jit(solution)/shard_map/all_to_all | solution.py:167
  247.8 28.7 %all-to-all-start.3 = ((bf16[4,128,1024]{2,1,0:T(8,128)(2,1)}), bf16[4,128,1024]{2,1,0:T(8,128)(2,1)S(1)}, u32[]{:S(2)}, u32[]{:S(2)}) async-start(bf16[4,128,1024]{2,1,0:T(8,128)(2,1)} %all_to_all.119), calls=%async_computation.3 | async-start | bytes 2097152 | tf_op jit(solution)/shard_map/all_to_all | solution.py:166
Sparse Core Ops, SparseCore 0:
  131.3 33.3 reduce-scatter.4
  168.7 33.5 reduce-scatter.2
where the time goes:
time: 286 us; the launch traced here: 285 us
  waiting for transfers between devices  128 us (45%)
  matrix products  45.5 us (16%)
  starting transfers between devices  33.5 us (12%)
  local copies, waits for them, and re-layouts  30.2 us (11%)
  blocking collectives  18.6 us (7%)
  other arithmetic  14.8 us (5%)
  between operations  14.4 us (5%)
    reduce_scatter x1, waiting for transfers between devices, local(): lax.psum_scatter(value_buffer.astype(jnp.bfloat16), 'ctx', scatter_dimens...  28.9 us
    reduce_scatter x1, waiting for transfers between devices, local(): lax.psum_scatter(key_buffer.astype(jnp.bfloat16), 'ctx', scatter_dimensio...  22.4 us
    all_to_all x1, waiting for transfers between devices, local(): lax.all_to_all(query_out, 'head', split_axis=0, concat_axis=1, tiled=True)  21.5 us
    all_to_all x1, waiting for transfers between devices, local(): lax.all_to_all(queries, 'head', split_axis=1, concat_axis=0, tiled=True)  20.7 us
    all_to_all x1, waiting for transfers between devices, local(): lax.all_to_all(attended_out, 'head', split_axis=0, concat_axis=1, tiled=T...  19.9 us
    all_gather x1, blocking collectives, local(): lax.all_gather(key_rows[positions], 'ctx', axis=0, tiled=True)  9.32 us
    all_gather x1, blocking collectives, local(): lax.all_gather(value_rows[positions], 'ctx', axis=0, tiled=True)  9.29 us
    all_to_all x1, waiting for transfers between devices, local(): lax.all_to_all(keys, 'head', split_axis=1, concat_axis=0, tiled=True)  7.25 us
  transfers between devices with their start and end apart: 10, of which 9 were waited for; matrix products, arithmetic and copies ran while one was open for 14% of the time, Pallas kernels for 0%

commit v1 on v0

--- a/solution.py
+++ b/solution.py
@@ -8,6 +8,19 @@
 
 
 def local(queries, keys, values, out_grad, beacon_pos):
+
+    def update_domain(shard_in):
+        seen_now = jnp.concatenate(
+            lax.all_to_all(
+                jnp.stack(jnp.split(shard_in, lax.axis_size("head"), 0), 0),
+                axis_name="head",
+                split_axis=0,
+                concat_axis=0,
+            ),
+            1,
+        )
+        return seen_now
+
     query_rows, key_rows, value_rows, grad_rows = (
         lax.all_to_all(queries, "head", split_axis=1, concat_axis=0, tiled=True),
         lax.all_to_all(keys, "head", split_axis=1, concat_axis=0, tiled=True),
@@ -163,7 +176,7 @@
     key_out = key_grad.astype(jnp.bfloat16).reshape(window, kv_local * HD)
     value_out = value_grad.astype(jnp.bfloat16).reshape(window, kv_local * HD)
     return (
-        lax.all_to_all(attended_out, "head", split_axis=0, concat_axis=1, tiled=True),
+        update_domain(attended_out),
         lax.all_to_all(query_out, "head", split_axis=0, concat_axis=1, tiled=True),
         lax.all_to_all(key_out, "head", split_axis=0, concat_axis=1, tiled=True),
         lax.all_to_all(value_out, "head", split_axis=0, concat_axis=1, tiled=True),

time: 286 us -> 265 us (0.927)
  waiting for transfers between devices: 128 us -> 92 us
  other arithmetic: 14.8 us -> 21.4 us
  local copies, waits for them, and re-layouts: 30.2 us -> 35.7 us
    reduce_scatter x1, waiting for transfers between devices: 28.9 us -> 0.02 us  [local(): lax.psum_scatter(value_buffer.astype(jnp.bfloat16), 'ctx', scatter_dimens...]
    all_to_all x1, waiting for transfers between devices: 20.7 us -> 0.01 us  [local(): lax.all_to_all(queries, 'head', split_axis=1, concat_axis=0, tiled=True)]
    all_to_all x1, waiting for transfers between devices: 0.65 us -> 13.5 us  [local(): lax.all_to_all(out_grad, 'head', split_axis=1, concat_axis=0, tiled=True)]
    unnamed x24 -> x39, local copies, waits for them, and re-layouts: 3.13 us -> 8.68 us
    dot_general x1, matrix products: 3.96 us -> 7.83 us  [local(): jnp.einsum('kgwv,vkd->wkgd', local_probs_low, value_heads, preferred_elem...]
    dot_general x1, matrix products: 2.19 us -> 5.24 us  [beacon_scores(): jnp.einsum('jahm,pam->ahjp', query_head_rows, key_tile_block, preferred_e...]
  transfers between devices with their start and end apart: 10 -> 10, of which waited for: 9 -> 7; matrix products, arithmetic and copies ran while one was open for 14% -> 30% of each run, Pallas kernels for 0% -> 0%
where the time goes in v1:
time: 265 us; the launch traced here: 264 us
  waiting for transfers between devices  92 us (35%)
  matrix products  47.4 us (18%)
  local copies, waits for them, and re-layouts  35.7 us (13%)
  starting transfers between devices  34.2 us (13%)
  other arithmetic  21.4 us (8%)
  blocking collectives  18.6 us (7%)
  between operations  14.5 us (5%)
    all_to_all x1, waiting for transfers between devices, local(): lax.all_to_all(query_out, 'head', split_axis=0, concat_axis=1, tiled=True)  22.8 us
    reduce_scatter x1, waiting for transfers between devices, local(): lax.psum_scatter(key_buffer.astype(jnp.bfloat16), 'ctx', scatter_dimensio...  21.7 us
    all_to_all x1, waiting for transfers between devices, update_domain(): lax.all_to_all(jnp.stack(jnp.split(shard_in, lax.axis_size('head'), 0), 0...  19.9 us
    all_to_all x1, waiting for transfers between devices, local(): lax.all_to_all(out_grad, 'head', split_axis=1, concat_axis=0, tiled=True)  13.5 us
    all_gather x1, blocking collectives, local(): lax.all_gather(key_rows[positions], 'ctx', axis=0, tiled=True)  9.32 us
    all_gather x1, blocking collectives, local(): lax.all_gather(value_rows[positions], 'ctx', axis=0, tiled=True)  9.29 us
    unnamed x39, local copies, waits for them, and re-layouts  8.68 us
    dot_general x1, matrix products, local(): jnp.einsum('wkgd,vkd->kgwv', head_gradients, value_heads, preferred_eleme...  8.24 us
  transfers between devices with their start and end apart: 10, of which 7 were waited for; matrix products, arithmetic and copies ran while one was open for 30% of the time, Pallas kernels for 0%

profile of v1, /device:TPU:0, one launch (start us, length us, event | category | flops | bytes accessed | tf_op | source)
XLA Modules:
  0.0 263.8 jit_solution(3502824906890383495)
XLA Ops:
  8.8 6.3 %all-to-all-start = ((bf16[128,4,256]{2,0,1:T(8,128)(2,1)}), bf16[128,4,256]{2,0,1:T(8,128)(2,1)S(1)}, u32[]{:S(2)}, u32[]{:S(2)}) async-start(bf16[128,4,256]{2,0,1:T(8,128)(2,1)} %bitcast.169), calls=%async_computation | async-start | bytes 524288 | tf_op jit(solution)/shard_map/all_to_all | solution.py:26
  17.0 7.1 %all-to-all-done = bf16[128,4,256]{2,0,1:T(8,128)(2,1)S(1)} async-done(((bf16[128,4,256]{2,0,1:T(8,128)(2,1)}), bf16[128,4,256]{2,0,1:T(8,128)(2,1)S(1)}, u32[]{:S(2)}, u32[]{:S(2)}) %all-to-all-start) | async-done | bytes 262176 | tf_op jit(solution)/shard_map/all_to_all | solution.py:26
  29.8 4.7 %all-to-all-done.2 = bf16[128,4,256]{0,2,1:T(8,128)(2,1)S(1)} async-done(((bf16[128,4,256]{0,2,1:T(8,128)(2,1)}), bf16[128,4,256]{0,2,1:T(8,128)(2,1)S(1)}, u32[]{:S(2)}, u32[]{:S(2)}) %all-to-all-start.2) | async-done | bytes 262176 | tf_op jit(solution)/shard_map/all_to_all | solution.py:27
  34.5 3.5 %all-to-all-start.1 = ((bf16[128,4,1024]{2,0,1:T(8,128)(2,1)}), bf16[128,4,1024]{2,0,1:T(8,128)(2,1)S(1)}, u32[]{:S(2)}, u32[]{:S(2)}) async-start(bf16[128,4,1024]{2,0,1:T(8,128)(2,1)} %bitcast.168), calls=%async_computation.1 | async-start | bytes 2097152 | tf_op jit(solution)/shard_map/all_to_all | solution.py:25
  44.5 9.3 %all-gather = bf16[512,256]{1,0:T(8,128)(2,1)S(1)} all-gather(bf16[64,256]{1,0:T(8,128)(2,1)S(1)} %gather_fusion), channel_id=2, replica_groups=mesh['ctx'=8,'head'=4] {'ctx'}, dimensions={0}, use_global_device_ids=true | all-gather | bytes 294912 | tf_op jit(solution)/shard_map/all_gather | solution.py:40
  54.7 9.3 %all-gather.1 = bf16[512,256]{1,0:T(8,128)(2,1)S(1)} all-gather(bf16[64,256]{1,0:T(8,128)(2,1)S(1)} %gather_fusion.1), channel_id=3, replica_groups=mesh['ctx'=8,'head'=4] {'ctx'}, dimensions={0}, use_global_device_ids=true | all-gather | bytes 294912 | tf_op jit(solution)/shard_map/all_gather | solution.py:41
  64.9 5.1 %all-to-all-start.4 = ((bf16[128,4,1024]{2,0,1:T(8,128)(2,1)}), bf16[128,4,1024]{2,0,1:T(8,128)(2,1)S(1)}, u32[]{:S(2)}, u32[]{:S(2)}) async-start(bf16[128,4,1024]{2,0,1:T(8,128)(2,1)} %bitcast.167), calls=%async_computation.4 | async-start | bytes 2097152 | tf_op jit(solution)/shard_map/all_to_all | solution.py:28
  70.7 5.2 %bitcast_reduce_fusion = (f32[2,4,512]{2,1,0:T(4,128)S(1)}, f32[2,512,512,4]{2,1,3,0:T(8,128)}) fusion(pred[512]{0:T(512)(128)(4,1)S(1)} %fusion.53, bf16[512,2,128,1]{0,2,3,1:T(8,128)(2,1)S(1)} %bitcast.186, bf16[512,2,4,128]{3,2,1,0:T(4,128)(2,1)S(1)} %reshape.120), kind=kOutput, calls=%fused_computation.11 | convolution fusion | flops 543158272 | bytes 9716224 | tf_op jit(solution)/shard_map/while/body/eval_jaxpr/jahm,pam->ahjp/dot_general | solution.py:64
  82.6 13.5 %all-to-all-done.4 = bf16[128,4,1024]{2,0,1:T(8,128)(2,1)S(1)} async-done(((bf16[128,4,1024]{2,0,1:T(8,128)(2,1)}), bf16[128,4,1024]{2,0,1:T(8,128)(2,1)S(1)}, u32[]{:S(2)}, u32[]{:S(2)}) %all-to-all-start.4) | async-done | bytes 1048608 | tf_op jit(solution)/shard_map/all_to_all | solution.py:28
  96.9 4.6 %fusion.7 = f32[2,4,512]{2,1,0:T(4,128)S(1)} fusion(f32[2,512,512,4]{2,1,3,0:T(8,128)} %get-tuple-element.101, f32[2,4,512]{2,1,0:T(4,128)S(1)} %max.11, pred[512]{0:T(512)(128)(4,1)S(1)} %fusion.53), kind=kLoop, calls=%fused_computation.19 | loop fusion | flops 8384512 | bytes 8421888 | tf_op jit(solution)/shard_map/while/body/eval_jaxpr/reduce_sum | solution.py:81
  101.5 4.8 %fusion.6 = f32[2,4,512,512]{2,3,1,0:T(8,128)S(1)} fusion(f32[2,512,512,4]{2,1,3,0:T(8,128)} %get-tuple-element.101, f32[2,4,512]{2,1,0:T(4,128)S(1)} %bitcast.204, f32[2,4,512]{2,1,0:T(4,128)S(1)} %max.11, pred[512]{0:T(512)(128)(4,1)S(1)} %fusion.53), kind=kLoop, calls=%fused_computation.18 | loop fusion | flops 8388608 | bytes 16810496 | tf_op jit(solution)/shard_map/while/body/eval_jaxpr/div | solution.py:89
  112.0 4.1 %fusion.13 = f32[2,128,4,512]{3,1,2,0:T(8,128)S(1)} fusion(bf16[512,2,128,1]{0,2,3,1:T(8,128)(2,1)S(1)} %bitcast.189, f32[2,4,512,512]{2,3,1,0:T(8,128)} %copy-done), kind=kOutput, calls=%fused_computation.28 | convolution fusion | flops 538968064 | bytes 10747904 | tf_op jit(solution)/shard_map/while/body/eval_jaxpr/lupa,alx->plux/dot_general | solution.py:100
  116.1 7.8 %bitcast_convert_fusion = (f32[2,4,512,128]{2,3,1,0:T(8,128)}, bf16[512,2,4,128]{0,3,2,1:T(8,128)(2,1)}) fusion(f32[2,128,4,512]{3,1,2,0:T(8,128)S(1)} %fusion.13, f32[2,4,512]{2,1,0:T(4,128)S(1)} %bitcast.206, f32[2,4,512]{2,1,0:T(4,128)S(1)} %max.11, f32[2,512,512,4]{2,1,3,0:T(8,128)} %copy-done.2, pred[512,512]{0,1:T(8,128)(4,1)S(1)} %copy-done.10, ...), kind=kOutput, calls=%fused_computation.48 | convolution fusion | flops 548929536 | bytes 14188544 | tf_op jit(solution)/shard_map/kgwv,vkd->wkgd/dot_general | solution.py:93
  130.0 4.8 %fusion.1 = bf16[2,4,512,512]{2,3,1,0:T(8,128)(2,1)S(1)} fusion(f32[2,4,512,512]{2,3,1,0:T(8,128)} %copy-done, f32[2,4,512]{2,1,0:T(4,128)S(1)} %copy.145, bf16[512,2,128,1]{0,2,3,1:T(8,128)(2,1)} %bitcast.188, bf16[512,2,4,128]{3,2,1,0:T(4,128)(2,1)S(1)} %reshape.126), kind=kOutput, calls=%fused_computation.6 | convolution fusion | flops 543162368 | bytes 13910016 | tf_op jit(solution)/shard_map/while/body/eval_jaxpr/jahm,pam->ahjp/dot_general | solution.py:133
  134.9 8.2 %fusion.3 = bf16[2,4,512,512]{2,3,1,0:T(8,128)(2,1)} fusion(f32[2,4,512]{2,1,0:T(4,128)S(1)} %copy.145, bf16[512,2,4,128]{3,2,1,0:T(4,128)(2,1)S(1)} %reshape.126, bf16[512,2,128]{0,2,1:T(8,128)(2,1)S(1)} %copy-done.13, f32[2,4,512]{2,1,0:T(4,128)S(1)} %bitcast.207, f32[2,4,512]{2,1,0:T(4,128)S(1)} %max.11, f32[2,512,512,4]{2,1,3,0:T(8,128)} %copy-done.2, ...), kind=kOutput, calls=%fused_computation.9 | convolution fusion | flops 551550976 | bytes 14204928 | tf_op jit(solution)/shard_map/wkgd,vkd->kgwv/dot_general | solution.py:111
  149.7 4.1 %all-to-all-start.7 = ((bf16[4,128,256]{2,1,0:T(8,128)(2,1)}), bf16[4,128,256]{2,1,0:T(8,128)(2,1)}, u32[]{:S(2)}, u32[]{:S(2)}) async-start(bf16[4,128,256]{2,1,0:T(8,128)(2,1)} %all_to_all.120), calls=%async_computation.9 | async-start | bytes 524288 | tf_op jit(solution)/shard_map/all_to_all | solution.py:182
  153.8 3.6 %fusion.28 = f32[512,2,128]{2,0,1:T(8,128)S(1)} fusion(bf16[2,4,512,512]{2,3,1,0:T(8,128)(2,1)} %fusion.3, bf16[512,2,4,128]{3,2,1,0:T(4,128)(2,1)S(1)} %copy-done.4), kind=kOutput, calls=%fused_computation.39 | convolution fusion | flops 537001984 | bytes 5767168 | tf_op jit(solution)/shard_map/kgwv,wkgd->vkd/dot_general | solution.py:119
  159.7 21.7 %reduce-scatter.3.cloned.1.call-done = bf16[64,2,128]{2,0,1:T(8,128)(2,1)} async-done(((bf16[512,2,128]{2,0,1:T(8,128)(2,1)}), bf16[64,2,128]{2,0,1:T(8,128)(2,1)}) %reduce-scatter.3.cloned.1.call-update) | async-done | bytes 32784 | tf_op jit(solution)/shard_map/reduce_scatter | solution.py:165
  186.0 4.7 %all-to-all-start.6 = ((bf16[4,128,256]{2,1,0:T(8,128)(2,1)}), bf16[4,128,256]{2,1,0:T(8,128)(2,1)}, u32[]{:S(2)}, u32[]{:S(2)}) async-start(bf16[4,128,256]{2,1,0:T(8,128)(2,1)} %all_to_all.116), calls=%async_computation.7 | async-start | bytes 524288 | tf_op jit(solution)/shard_map/all_to_all | solution.py:181
  190.7 3.9 %fusion.9 = bf16[512,2,4,128]{3,0,2,1:T(8,128)(2,1)S(1)} fusion(f32[2,4,512,128]{3,2,1,0:T(8,128)S(1)} %fusion.50, bf16[512,2,128,1]{0,2,3,1:T(8,128)(2,1)S(1)} %bitcast.187, bf16[2,4,512,512]{2,3,1,0:T(8,128)(2,1)} %copy-done.1), kind=kOutput, calls=%fused_computation.22 | convolution fusion | flops 538443776 | bytes 7602176 | tf_op jit(solution)/shard_map/while/body/eval_jaxpr/lupa,alx->plux/dot_general | solution.py:137
  199.2 3.5 %all-to-all-start.5 = ((bf16[4,128,1024]{2,1,0:T(8,128)(2,1)}), bf16[4,128,1024]{2,1,0:T(8,128)(2,1)S(1)}, u32[]{:S(2)}, u32[]{:S(2)}) async-start(bf16[4,128,1024]{2,1,0:T(8,128)(2,1)} %all_to_all.112), calls=%async_computation.5 | async-start | bytes 2097152 | tf_op jit(solution)/shard_map/all_to_all | solution.py:180
  204.2 22.8 %all-to-all-done.5 = bf16[4,128,1024]{2,1,0:T(8,128)(2,1)S(1)} async-done(((bf16[4,128,1024]{2,1,0:T(8,128)(2,1)}), bf16[4,128,1024]{2,1,0:T(8,128)(2,1)S(1)}, u32[]{:S(2)}, u32[]{:S(2)}) %all-to-all-start.5) | async-done | bytes 1048608 | tf_op jit(solution)/shard_map/all_to_all | solution.py:180
  226.9 3.5 %all-to-all-start.3 = ((bf16[4,128,1024]{1,2,0:T(8,128)(2,1)}), bf16[4,128,1024]{1,2,0:T(8,128)(2,1)S(1)}, u32[]{:S(2)}, u32[]{:S(2)}) async-start(bf16[4,128,1024]{1,2,0:T(8,128)(2,1)} %pad_maximum_fusion), calls=%async_computation.3 | async-start | bytes 2097152 | tf_op jit(solution)/shard_map/all_to_all | solution.py:14
  235.8 19.9 %all-to-all-done.3 = bf16[4,128,1024]{1,2,0:T(8,128)(2,1)S(1)} async-done(((bf16[4,128,1024]{1,2,0:T(8,128)(2,1)}), bf16[4,128,1024]{1,2,0:T(8,128)(2,1)S(1)}, u32[]{:S(2)}, u32[]{:S(2)}) %all-to-all-start.3) | async-done | bytes 1048608 | tf_op jit(solution)/shard_map/all_to_all | solution.py:14
  (95 shorter events, 63.1 us)
Async XLA Ops:
  7.2 33.2 %copy-start.15 = (s32[1,64]{1,0:T(1,128)S(1)}, s32[1,64]{1,0:T(1,128)}, u32[]{:S(2)}) copy-start(s32[1,64]{1,0:T(1,128)} %param.9) | copy-start | bytes 772
  8.8 15.2 %all-to-all-start = ((bf16[128,4,256]{2,0,1:T(8,128)(2,1)}), bf16[128,4,256]{2,0,1:T(8,128)(2,1)S(1)}, u32[]{:S(2)}, u32[]{:S(2)}) async-start(bf16[128,4,256]{2,0,1:T(8,128)(2,1)} %bitcast.169), calls=%async_computation | async-start | bytes 524288 | tf_op jit(solution)/shard_map/all_to_all | solution.py:26
  24.1 10.4 %all-to-all-start.2 = ((bf16[128,4,256]{0,2,1:T(8,128)(2,1)}), bf16[128,4,256]{0,2,1:T(8,128)(2,1)S(1)}, u32[]{:S(2)}, u32[]{:S(2)}) async-start(bf16[128,4,256]{0,2,1:T(8,128)(2,1)} %bitcast.12), calls=%async_computation.2 | async-start | bytes 524288 | tf_op jit(solution)/shard_map/all_to_all | solution.py:27
  34.5 30.4 %all-to-all-start.1 = ((bf16[128,4,1024]{2,0,1:T(8,128)(2,1)}), bf16[128,4,1024]{2,0,1:T(8,128)(2,1)S(1)}, u32[]{:S(2)}, u32[]{:S(2)}) async-start(bf16[128,4,1024]{2,0,1:T(8,128)(2,1)} %bitcast.168), calls=%async_computation.1 | async-start | bytes 2097152 | tf_op jit(solution)/shard_map/all_to_all | solution.py:25
  64.9 31.3 %all-to-all-start.4 = ((bf16[128,4,1024]{2,0,1:T(8,128)(2,1)}), bf16[128,4,1024]{2,0,1:T(8,128)(2,1)S(1)}, u32[]{:S(2)}, u32[]{:S(2)}) async-start(bf16[128,4,1024]{2,0,1:T(8,128)(2,1)} %bitcast.167), calls=%async_computation.4 | async-start | bytes 2097152 | tf_op jit(solution)/shard_map/all_to_all | solution.py:28
  69.9 75.2 %reduce-scatter.5.cloned.1.call-start = ((), (), s32[]{:S(2)}) async-start(), calls=%async_computation.11 | async-start | bytes 294912 | tf_op jit(solution)/shard_map/reduce_scatter | solution.py:168
  70.7 7.0 %copy-start.3 = (bf16[512,2,4,128]{3,2,1,0:T(4,128)(2,1)}, bf16[512,2,4,128]{3,2,1,0:T(4,128)(2,1)S(1)}, u32[]{:S(2)}) copy-start(bf16[512,2,4,128]{3,2,1,0:T(4,128)(2,1)S(1)} %reshape.120) | copy-start | bytes 3145732
  70.7 5.3 %copy-start.8 = (bf16[512,2,128]{2,1,0:T(2,128)(2,1)S(1)}, bf16[512,2,128]{2,1,0:T(2,128)(2,1)}, u32[]{:S(2)}) copy-start(bf16[512,2,128]{2,1,0:T(2,128)(2,1)} %reshape.119) | copy-start | bytes 786436
  70.7 5.3 %copy-start.10 = (pred[512,512]{0,1:T(8,128)(4,1)S(1)}, pred[512,512]{0,1:T(8,128)(4,1)}, u32[]{:S(2)}) copy-start(pred[512,512]{0,1:T(8,128)(4,1)} %iota_compare_fusion) | copy-start | bytes 786436
  96.9 9.5 %slice-start = ((s8[8388608]{0:T(1024)(128)(4,1)}), s8[4194304]{0:T(1024)(128)(4,1)S(1)}, s32[]{:S(2)}) async-start(s8[8388608]{0:T(1024)(128)(4,1)} %bitcast.175), calls=%async_computation.12 | async-start | bytes 8388608
  101.5 4.9 %slice-start.1 = ((s8[8388608]{0:T(1024)(128)(4,1)}), s8[4194304]{0:T(1024)(128)(4,1)S(1)}, s32[]{:S(2)}) async-start(s8[8388608]{0:T(1024)(128)(4,1)} %bitcast.175), calls=%async_computation.13 | async-start | bytes 8388608
  109.9 6.2 %copy-start.14 = (bf16[512,2,128,1]{0,2,1,3:T(8,128)(2,1)S(1)}, bf16[512,2,128,1]{0,2,1,3:T(8,128)(2,1)}, u32[]{:S(2)}) copy-start(bf16[512,2,128,1]{0,2,1,3:T(8,128)(2,1)} %reshape.163) | copy-start | bytes 786436
  111.9 69.4 %reduce-scatter.3.cloned.1.call-start = ((), (), s32[]{:S(2)}) async-start(), calls=%async_computation.10 | async-start | bytes 294912 | tf_op jit(solution)/shard_map/reduce_scatter | solution.py:165
  128.7 6.1 %copy-start.11 = (pred[512,512]{0,1:T(8,128)(4,1)S(1)}, pred[512,512]{0,1:T(8,128)(4,1)}, u32[]{:S(2)}) copy-start(pred[512,512]{0,1:T(8,128)(4,1)} %iota_compare_fusion) | copy-start | bytes 786436
  128.7 6.1 %copy-start.13 = (bf16[512,2,128]{0,2,1:T(8,128)(2,1)S(1)}, bf16[512,2,128]{0,2,1:T(8,128)(2,1)}, u32[]{:S(2)}) copy-start(bf16[512,2,128]{0,2,1:T(8,128)(2,1)} %reshape.122) | copy-start | bytes 786436
  134.8 8.3 %copy-start.1 = (bf16[2,4,512,512]{2,3,1,0:T(8,128)(2,1)}, bf16[2,4,512,512]{2,3,1,0:T(8,128)(2,1)S(1)}, u32[]{:S(2)}) copy-start(bf16[2,4,512,512]{2,3,1,0:T(8,128)(2,1)S(1)} %fusion.1) | copy-start | bytes 12582916
  134.8 8.3 %copy-start.4 = (bf16[512,2,4,128]{3,2,1,0:T(4,128)(2,1)S(1)}, bf16[512,2,4,128]{3,2,1,0:T(4,128)(2,1)}, u32[]{:S(2)}) copy-start(bf16[512,2,4,128]{3,2,1,0:T(4,128)(2,1)} %copy-done.3) | copy-start | bytes 3145732
  134.9 11.1 %copy-start.6 = (f32[512,2,128]{2,1,0:T(2,128)S(1)}, f32[512,2,128]{2,1,0:T(2,128)}, u32[]{:S(2)}) copy-start(f32[512,2,128]{2,1,0:T(2,128)} %copy.128) | copy-start | bytes 1572868
  143.1 14.7 %copy-start.9 = (bf16[512,2,128]{2,1,0:T(2,128)(2,1)S(1)}, bf16[512,2,128]{2,1,0:T(2,128)(2,1)}, u32[]{:S(2)}) copy-start(bf16[512,2,128]{2,1,0:T(2,128)(2,1)} %reshape.119) | copy-start | bytes 786436
  149.7 36.2 %all-to-all-start.7 = ((bf16[4,128,256]{2,1,0:T(8,128)(2,1)}), bf16[4,128,256]{2,1,0:T(8,128)(2,1)}, u32[]{:S(2)}, u32[]{:S(2)}) async-start(bf16[4,128,256]{2,1,0:T(8,128)(2,1)} %all_to_all.120), calls=%async_computation.9 | async-start | bytes 524288 | tf_op jit(solution)/shard_map/all_to_all | solution.py:182
  186.0 16.8 %copy-start.12 = (bf16[512,2,4,128]{0,3,2,1:T(8,128)(2,1)S(1)}, bf16[512,2,4,128]{0,3,2,1:T(8,128)(2,1)}, u32[]{:S(2)}) copy-start(bf16[512,2,4,128]{0,3,2,1:T(8,128)(2,1)} %get-tuple-element.103) | copy-start | bytes 3145732
  186.0 13.2 %all-to-all-start.6 = ((bf16[4,128,256]{2,1,0:T(8,128)(2,1)}), bf16[4,128,256]{2,1,0:T(8,128)(2,1)}, u32[]{:S(2)}, u32[]{:S(2)}) async-start(bf16[4,128,256]{2,1,0:T(8,128)(2,1)} %all_to_all.116), calls=%async_computation.7 | async-start | bytes 524288 | tf_op jit(solution)/shard_map/all_to_all | solution.py:181
  199.2 27.7 %all-to-all-start.5 = ((bf16[4,128,1024]{2,1,0:T(8,128)(2,1)}), bf16[4,128,1024]{2,1,0:T(8,128)(2,1)S(1)}, u32[]{:S(2)}, u32[]{:S(2)}) async-start(bf16[4,128,1024]{2,1,0:T(8,128)(2,1)} %all_to_all.112), calls=%async_computation.5 | async-start | bytes 2097152 | tf_op jit(solution)/shard_map/all_to_all | solution.py:180
  226.9 28.7 %all-to-all-start.3 = ((bf16[4,128,1024]{1,2,0:T(8,128)(2,1)}), bf16[4,128,1024]{1,2,0:T(8,128)(2,1)S(1)}, u32[]{:S(2)}, u32[]{:S(2)}) async-start(bf16[4,128,1024]{1,2,0:T(8,128)(2,1)} %pad_maximum_fusion), calls=%async_computation.3 | async-start | bytes 2097152 | tf_op jit(solution)/shard_map/all_to_all | solution.py:14
  (4 other events, 14.1 us)
Sparse Core Ops, SparseCore 0:
  112.1 31.7 reduce-scatter.4
  147.7 33.5 reduce-scatter.2
